TPU v7x, 512 devices: a whole 4x4x16 slice. The times are simulated.
512 devices in a mesh: space: 32 (over x, y, z_hi), tm: 16 (over z_lo, core).
Axes of the slice: x: 4, y: 4, z: 16 (z_hi: 2, z_lo: 8; z = z_hi * 8 + z_lo), core: 2. Of those that a mesh axis runs over, the one named last changes fastest.
Arguments:
- lattice_field: float32 [64, 128, 2048], P('tm', 'space'), may hold values from -6 to 6
- parity: int32 [16, 32, 128], P('tm', 'space'), may hold values from 0 to 1
- block_list: int32 [16, 8], replicated, may hold values from 0 to 15, as said below
- w_embed: bfloat16 [256, 768], replicated, may hold values from -0.5 to 0.5
- b_embed: float32 [768], replicated, may hold values from -3 to 3
- gain_in: float32 [768], replicated, may hold values from 0.5 to 1.5
- w_qkv: bfloat16 [768, 2304], replicated, may hold values from -4 to 4
- gain_out: float32 [768], replicated, may hold values from 0.5 to 1.5
- w_head: bfloat16 [768, 512], replicated, may hold values from -0.21875 to 0.21875
- b_head: float32 [512], replicated, may hold values from -3 to 3
Outputs:
- new_field: float32 [64, 128, 2048], P('tm', 'space')
- action_density: float32 [64, 128, 2048], P('tm', 'space')
- time_link: float32 [64, 128, 2048], P('tm', 'space')
- slab_link: float32 [64, 128, 2048], P('tm', 'space')
- totals: float32 [2], replicated
Inputs may be any that keep to these rules, and one draw needn't show every extreme that they name: `block_list`: row b lists 8 different block numbers, b among them.
All inputs are finite; a program needn't handle non-finite values.
Results may differ from a plain program's by a relative error of at most 0.006.
Values may be sent and summed in bfloat16 or wider, within the bound.
No kernel may reach another device: no remote copies, remote signals or barrier semaphores. Data moves between devices by JAX's collectives and lax.ppermute only.
A program may use at most 64 MiB of HBM per device.

v0:
```python
import math
import jax
import jax.numpy as jnp
from jax import lax
from jax.sharding import PartitionSpec as P

P_SIZE = 4
D = 768
HEADS = 12
HS = 64
LY = 32
LZ = 64
BLK = 128
hopping = 0.2
quartic = 0.5
epsilon = 1e-05
log_two_pi = math.log(2.0 * math.pi)
floor_score = -1e30


def shifted(x, axis, by):
    length = lax.axis_size(axis)
    return lax.ppermute(x, axis, [(i, (i + by) % length) for i in range(length)])


def layer_norm(values, gain_vec):
    centre = values - jnp.mean(values, axis=-1, keepdims=True)
    spread = jnp.mean(centre * centre, axis=-1, keepdims=True)
    return centre * lax.rsqrt(spread + epsilon) * gain_vec


def site_parity(patch_side):
    positions = jnp.arange(patch_side**4, dtype=jnp.int32)
    return (
        positions // patch_side**3
        + positions // patch_side**2 % patch_side
        + positions // patch_side % patch_side
        + positions % patch_side
    ) % 2


def embed_rows(frozen_in, w_embed, b_embed, gain_in):
    embedded = jnp.dot(frozen_in, w_embed, preferred_element_type=jnp.float32) + b_embed
    return (embedded, layer_norm(embedded, gain_in).astype(jnp.bfloat16))


def attend(carry_in, queries, key_part, value_part, first_key, block_rows):
    running_max, running_sum, running_out = carry_in
    key_rows = key_part.shape[0]
    key_block = (first_key + jnp.arange(key_rows, dtype=jnp.int32)) // BLK
    listed = jnp.any(block_rows[:, :, None] == key_block[None, None, :], axis=1)
    allowed = jnp.repeat(listed, BLK, axis=0)[None]
    query_heads = queries.reshape(queries.shape[0], HEADS, HS)
    scores = jnp.einsum(
        "qhd,khd->hqk",
        query_heads,
        key_part.reshape(key_rows, HEADS, HS),
        preferred_element_type=jnp.float32,
    ) * HS ** (-0.5)
    masked = jnp.where(allowed, scores, floor_score)
    new_max = jnp.maximum(running_max, jnp.max(masked, axis=2))
    exp_scores = jnp.where(allowed, jnp.exp(scores - new_max[:, :, None]), 0.0)
    factor = jnp.exp(running_max - new_max)
    running_sum = running_sum * factor + jnp.sum(exp_scores, axis=2)
    product = jnp.einsum(
        "hqk,khd->hqd",
        exp_scores.astype(jnp.bfloat16),
        value_part.reshape(key_rows, HEADS, HS),
        preferred_element_type=jnp.float32,
    )
    running_out = running_out * factor[:, :, None] + product
    return (new_max, running_sum, running_out)


def fold_rows(carry_in, pieces_in, make_pair, queries, block_rows):
    row_total = pieces_in[0].shape[0]
    pieces_split = tuple(
        (
            piece_arr.reshape((row_total // BLK, BLK) + piece_arr.shape[1:])
            for piece_arr in pieces_in
        )
    )

    def visit_block(carry_now, item_pair):
        position, block_parts = item_pair
        first_key = position * BLK
        block_id = first_key // BLK
        needed = jnp.any(block_rows == block_id)

        def compute_block(carry_here):
            key_part, value_part = make_pair(block_parts)
            return attend(carry_here, queries, key_part, value_part, first_key, block_rows)

        def skip_block(carry_here):
            return carry_here

        return (lax.cond(needed, compute_block, skip_block, carry_now), None)

    carry_out, _ = lax.scan(
        visit_block, carry_in, (jnp.arange(row_total // BLK, dtype=jnp.int32), pieces_split)
    )
    return carry_out


def shards(
    lattice_field, parity, block_list, w_embed, b_embed, gain_in, w_qkv, gain_out, w_head, b_head
):
    tokens_dev = LY // P_SIZE * (LZ // P_SIZE)
    patch_len = P_SIZE**4
    lattice_grid = lattice_field.reshape(
        P_SIZE, P_SIZE, LY // P_SIZE, P_SIZE, LZ // P_SIZE, P_SIZE
    ).transpose(2, 4, 0, 1, 3, 5)
    site_rows = lattice_grid.reshape(tokens_dev, patch_len)
    frozen = site_parity(P_SIZE)[None, :] == parity.reshape(tokens_dev)[:, None]
    frozen_in = jnp.where(frozen, site_rows, 0.0).astype(jnp.bfloat16)
    embedded, normed = embed_rows(frozen_in, w_embed, b_embed, gain_in)
    blocks_dev = tokens_dev // BLK
    block_rows = lax.dynamic_slice_in_dim(
        block_list, lax.axis_index("tm") * blocks_dev, blocks_dev, 0
    )
    start_state = (
        jnp.full((HEADS, tokens_dev), floor_score, jnp.float32),
        jnp.zeros((HEADS, tokens_dev), jnp.float32),
        jnp.zeros((HEADS, tokens_dev, HS), jnp.float32),
    )
    qkv_rows = jnp.dot(normed, w_qkv, preferred_element_type=jnp.float32).astype(jnp.bfloat16)
    queries = qkv_rows[:, :D]

    def from_pair(block_parts):
        return (block_parts[0], block_parts[1])

    result = fold_rows(
        start_state,
        (
            lax.all_gather(qkv_rows[:, D : 2 * D], "tm", axis=0, tiled=True),
            lax.all_gather(qkv_rows[:, 2 * D :], "tm", axis=0, tiled=True),
        ),
        from_pair,
        queries,
        block_rows,
    )
    _, running_sum, running_out = result
    mixed = (running_out / running_sum[:, :, None]).transpose(1, 0, 2).reshape(tokens_dev, D)
    hidden = embedded + mixed
    normed_out = layer_norm(hidden, gain_out).astype(jnp.bfloat16)
    affine = jnp.dot(normed_out, w_head, preferred_element_type=jnp.float32) + b_head
    scale_log = jnp.tanh(affine[:, :patch_len])
    shift_val = affine[:, patch_len:]
    moved = jnp.where(frozen, site_rows, site_rows * jnp.exp(scale_log) + shift_val)
    log_det = jnp.sum(jnp.where(frozen, 0.0, scale_log))
    new_field = (
        moved.reshape(LY // P_SIZE, LZ // P_SIZE, P_SIZE, P_SIZE, P_SIZE, P_SIZE)
        .transpose(2, 3, 0, 4, 1, 5)
        .reshape(P_SIZE, P_SIZE, LY * LZ)
    )
    ahead_time = shifted(new_field[0:1].astype(jnp.bfloat16), "tm", -1).astype(jnp.float32)
    ahead_slab = shifted(new_field[:, 0:1].astype(jnp.bfloat16), "space", -1).astype(jnp.float32)
    next_time_field = jnp.concatenate([new_field[1:], ahead_time], axis=0)
    next_slab_field = jnp.concatenate([new_field[:, 1:], ahead_slab], axis=1)
    cube = new_field.reshape(P_SIZE, P_SIZE, LY, LZ)
    next_y_field = jnp.roll(cube, -1, 2).reshape(P_SIZE, P_SIZE, LY * LZ)
    next_z_field = jnp.roll(cube, -1, 3).reshape(P_SIZE, P_SIZE, LY * LZ)
    neighbours = next_time_field + next_slab_field
    neighbours = neighbours + next_y_field
    neighbours = neighbours + next_z_field
    squared = new_field * new_field
    density = (
        -2.0 * hopping * new_field * neighbours
        + squared
        + quartic * (squared - 1.0) * (squared - 1.0)
    )
    time_link = new_field * next_time_field
    slab_link = new_field * next_slab_field
    local_log = -0.5 * jnp.sum(lattice_field * lattice_field) - log_det
    local_act = jnp.sum(density)
    sum_log, sum_act = lax.psum((local_log, local_act), ("space", "tm"))
    site_count = lattice_field.size * lax.axis_size("space") * lax.axis_size("tm")
    totals = jnp.stack([sum_log / site_count - 0.5 * log_two_pi, sum_act / site_count]).astype(
        jnp.float32
    )
    return (new_field, density, time_link, slab_link, totals)


def solution(mesh):
    in_specs = (
        P("tm", "space", None),
        P("tm", "space", None),
        P(),
        P(),
        P(),
        P(),
        P(),
        P(),
        P(),
        P(),
    )
    out_specs = (
        P("tm", "space", None),
        P("tm", "space", None),
        P("tm", "space", None),
        P("tm", "space", None),
        P(),
    )
    return jax.shard_map(shards, mesh=mesh, in_specs=in_specs, out_specs=out_specs, check_vma=False)
```

profile of v0, /device:TPU:1, one launch (start us, length us, event | category | flops | bytes accessed | tf_op | source)
XLA Modules:
  0.0 584.1 jit_solution(14701347401462404792)
XLA Ops:
  7.3 6.7 %reshape.277 = f32[4,4,8,4,16,4]{5,4,3,2,1,0:T(8,128)} reshape(f32[4,4,2048]{2,1,0:T(4,128)} %param.14) | data formatting | bytes 262144 | tf_op jit(solution)/shard_map/reshape | solution.py:110
  14.0 5.7 copy.50
  19.6 2.2 reshape.278
  28.6 1.7 copy.54
  32.6 102.8 %all-gather.3.cloned.1.call-done = bf16[2048,768]{1,0:T(8,128)(2,1)} async-done(((bf16[128,768]{1,0:T(8,128)(2,1)}), bf16[2048,768]{1,0:T(8,128)(2,1)}) %all-gather.3.cloned.1.call-update) | async-done | bytes 3145744 | tf_op jit(solution)/shard_map/all_gather | solution.py:135
  135.4 4.6 copy.53
  140.0 101.0 %all-gather.5.cloned.1.call-done = bf16[2048,768]{1,0:T(8,128)(2,1)} async-done(((bf16[128,768]{1,0:T(8,128)(2,1)}), bf16[2048,768]{1,0:T(8,128)(2,1)}) %all-gather.5.cloned.1.call-update) | async-done | bytes 3145744 | tf_op jit(solution)/shard_map/all_gather | solution.py:136
  241.0 4.7 copy.55
  247.1 100.4 %while.16 = (s32[]{:T(128)}, f32[12,128]{1,0:T(8,128)S(1)}, f32[12,128]{1,0:T(8,128)S(1)}, f32[12,128,64]{1,2,0:T(8,128)}, s32[16]{0:T(128)}, /*index=5*/s32[1,8...) while((s32[]{:T(128)}, f32[12,128]{1,0:T(8,128)S(1)}, ...), condition=%wide.region_9.10_spmd, body=%wide.region_2.9_spmd.sunk | while | flops 52304800 | bytes 7768141 | solution.py:99
  251.1 4.5 conditional.2
  259.6 4.5 conditional.2
  268.1 4.5 conditional.2
  280.6 4.5 conditional.2
  293.2 4.5 conditional.2
  301.7 4.5 conditional.2
  314.2 4.5 conditional.2
  338.9 4.5 conditional.2
  347.5 1.8 broadcast_divide_fusion
  349.3 1.9 copy.56
  354.1 2.2 fusion.18
  358.0 2.2 reshape.282
  360.2 5.4 copy.60
  365.7 5.6 reshape.283
  371.3 4.3 reshape_reshape.3
  375.5 1.8 slice.74
  383.6 9.5 %collective-permute-start.1 = (bf16[4,1,2048]{2,1,0:T(2,128)(2,1)}, bf16[4,1,2048]{2,1,0:T(2,128)(2,1)}, u32[]{:S(2)}, u32[]{:S(2)}) collective-permute-start(bf16[4,1,2048]{2,1,0:T(2,128)(2,1)} %slice.87), channel_id=1, source_target_pairs={{0,496},{16,0},{32,16},{48,32},{64,48},{80,64},{96,80},{112,96},{1... | collective-permute-start | bytes 49160 | tf_op jit(solution)/shard_map/ppermute | solution.py:23
  393.1 2.5 copy.62
  395.6 2.4 convert_element_type.46
  398.0 9.9 %collective-permute-start = (bf16[1,4,2048]{2,1,0:T(4,128)(2,1)}, bf16[1,4,2048]{2,1,0:T(4,128)(2,1)S(1)}, u32[]{:S(2)}, u32[]{:S(2)}) collective-permute-start(bf16[1,4,2048]{2,1,0:T(4,128)(2,1)} %convert_element_type.46), channel_id=1, source_target_pairs={{0,15},{1,0},{2,1},{3,2},{4,3},{5,4},{6,5},{7,6},{8,7},{9,8},{10,9... | collective-permute-start | bytes 49160 | tf_op jit(solution)/shard_map/ppermute | solution.py:23
  407.9 1.9 pad_maximum_fusion.1
  413.1 2.1 slice.68
  415.2 1.7 reshape.285
  416.9 4.4 reshape.287
  421.3 1.7 reshape.284
  423.1 4.5 reshape.286
  427.6 4.6 copy.61
  432.2 5.7 copy.69
  437.8 5.6 copy.68
  443.5 5.1 reshape.288
  448.6 4.6 copy.66
  453.9 2.1 concatenate.30
  455.9 2.8 copy.64
  460.2 2.8 concatenate.33
  463.0 2.8 copy.67
  465.8 3.7 fusion.5
  469.5 4.6 slice.55
  474.1 98.3 %all-reduce = (f32[]{:T(128)}, f32[]{:T(128)}) all-reduce(f32[]{:T(128)} %fusion.5, f32[]{:T(128)S(6)} %sub.78), channel_id=1, replica_groups=mesh['space'=32,'tm'=16] {'space','tm'}, use_global_device_ids=true, to_apply=%region_16.17 | all-reduce | flops 2 | bytes 16 | tf_op jit(solution)/shard_map/psum | solution.py:176
  575.2 2.1 fusion.20
  (201 shorter events, 104.5 us)
Async XLA Ops:
  7.2 18.5 %copy-start = (bf16[768,2304]{1,0:T(8,128)(2,1)S(1)}, bf16[768,2304]{1,0:T(8,128)(2,1)}, u32[]{:S(2)}) copy-start(bf16[768,2304]{1,0:T(8,128)(2,1)} %param.20) | copy-start | bytes 10616836
  7.2 128.2 %all-gather.3.cloned.1.call-start = ((), (), s32[]{:S(2)}) async-start(), calls=%async_computation | async-start | bytes 3342336 | tf_op jit(solution)/shard_map/all_gather | solution.py:135
  7.2 16.2 %copy-start.6 = (s32[256]{0:T(256)}, s32[256]{0:T(256)S(1)}, u32[]{:S(2)}) copy-start(s32[256]{0:T(256)S(1)} %and_select_fusion.1) | copy-start | bytes 3076
  14.0 9.5 %copy-start.4 = (f32[768]{0:T(1024)S(1)}, f32[768]{0:T(1024)}, u32[]{:S(2)}) copy-start(f32[768]{0:T(1024)} %param.18) | copy-start | bytes 9220
  14.0 9.5 %copy-start.10 = (s32[1,1,128]{2,1,0:T(1,128)S(1)}, s32[1,1,128]{2,1,0:T(1,128)}, u32[]{:S(2)}) copy-start(s32[1,1,128]{2,1,0:T(1,128)} %param.15) | copy-start | bytes 1540
  14.0 11.7 %copy-start.9 = (f32[768]{0:T(1024)S(1)}, f32[768]{0:T(1024)}, u32[]{:S(2)}) copy-start(f32[768]{0:T(1024)} %param.19) | copy-start | bytes 9220
  24.9 0.7 copy-start.3
  25.1 2.9 copy-start.8
  27.2 213.8 %all-gather.5.cloned.1.call-start = ((), (), s32[]{:S(2)}) async-start(), calls=%async_computation.1 | async-start | bytes 3342336 | tf_op jit(solution)/shard_map/all_gather | solution.py:136
  251.1 3.3 copy-start.1
  254.8 0.8 copy-start.2
  259.6 3.3 copy-start.1
  263.3 0.8 copy-start.2
  268.1 3.3 copy-start.1
  271.8 0.8 copy-start.2
  280.6 3.4 copy-start.1
  284.3 0.8 copy-start.2
  293.2 3.4 copy-start.1
  296.9 0.8 copy-start.2
  301.7 3.3 copy-start.1
  305.4 0.8 copy-start.2
  314.2 3.4 copy-start.1
  317.9 0.8 copy-start.2
  339.0 3.3 copy-start.1
  342.7 0.8 copy-start.2
  347.5 5.2 copy-start.5
  347.5 6.6 %copy-start.7 = (s32[256]{0:T(256)S(1)}, s32[256]{0:T(256)}, u32[]{:S(2)}) copy-start(s32[256]{0:T(256)} %copy-done.6) | copy-start | bytes 3076
  349.3 4.9 copy-start.11
  383.6 75.1 %collective-permute-start.1 = (bf16[4,1,2048]{2,1,0:T(2,128)(2,1)}, bf16[4,1,2048]{2,1,0:T(2,128)(2,1)}, u32[]{:S(2)}, u32[]{:S(2)}) collective-permute-start(bf16[4,1,2048]{2,1,0:T(2,128)(2,1)} %slice.87), channel_id=1, source_target_pairs={{0,496},{16,0},{32,16},{48,32},{64,48},{80,64},{96,80},{112,96},{1... | collective-permute-start | bytes 49160 | tf_op jit(solution)/shard_map/ppermute | solution.py:23
  398.0 55.8 %collective-permute-start = (bf16[1,4,2048]{2,1,0:T(4,128)(2,1)}, bf16[1,4,2048]{2,1,0:T(4,128)(2,1)S(1)}, u32[]{:S(2)}, u32[]{:S(2)}) collective-permute-start(bf16[1,4,2048]{2,1,0:T(4,128)(2,1)} %convert_element_type.46), channel_id=1, source_target_pairs={{0,15},{1,0},{2,1},{3,2},{4,3},{5,4},{6,5},{7,6},{8,7},{9,8},{10,9... | collective-permute-start | bytes 49160 | tf_op jit(solution)/shard_map/ppermute | solution.py:23
Sparse Core Ops, SparseCore 0:
  27.3 107.9 all-gather.2
  137.5 103.5 all-gather.4
where the time goes:
time: 587 us; the launch traced here: 584 us
  waiting for transfers between devices  205 us (35%)
  local copies, waits for them, and re-layouts  157 us (27%)
  blocking collectives  98.3 us (17%)
  other arithmetic  49 us (8%)
  loops' own time  22.7 us (4%)
  starting transfers between devices  19.5 us (3%)
  between operations  16.9 us (3%)
  matrix products  16.2 us (3%)
    all_gather x1, waiting for transfers between devices, shards(): lax.all_gather(qkv_rows[:, D:2 * D], 'tm', axis=0, tiled=True)  103 us
    all_gather x1, waiting for transfers between devices, shards(): lax.all_gather(qkv_rows[:, 2 * D:], 'tm', axis=0, tiled=True)  101 us
    psum x1, blocking collectives, shards(): sum_log, sum_act = lax.psum((local_log, local_act), ('space', 'tm'))  98.3 us
    dynamic_slice x24, local copies, waits for them, and re-layouts, fold_rows(): lax.scan(visit_block, carry_in, (jnp.arange(row_total // BLK, dtype=jnp.i...  29.4 us
    another operation x1, loops' own time, fold_rows(): lax.scan(visit_block, carry_in, (jnp.arange(row_total // BLK, dtype=jnp.i...  21.8 us
    reduce_or x16, other arithmetic, visit_block(): needed = jnp.any(block_rows == block_id)  21.6 us
    ppermute x2, starting transfers between devices, shifted(): lax.ppermute(x, axis, [(i, (i + by) % length) for i in range(length)])  19.4 us
    concatenate x4, local copies, waits for them, and re-layouts, shards(): next_slab_field = jnp.concatenate([new_field[:, 1:], ahead_slab], axis=1)  15.3 us
  transfers between devices with their start and end apart: 4, of which 2 were waited for; matrix products, arithmetic and copies ran while one was open for 11% of the time, Pallas kernels for 0%

commit v1 on v0

--- a/solution.py
+++ b/solution.py
@@ -133,7 +133,10 @@
         start_state,
         (
             lax.all_gather(qkv_rows[:, D : 2 * D], "tm", axis=0, tiled=True),
-            lax.all_gather(qkv_rows[:, 2 * D :], "tm", axis=0, tiled=True),
+            jnp.concatenate(
+                lax.all_to_all(jnp.stack([qkv_rows[:, 2 * D :]] * lax.axis_size("tm")), "tm", 0, 0),
+                axis=0,
+            ),
         ),
         from_pair,
         queries,

time: 587 us -> 565 us (0.963)
  waiting for transfers between devices: 205 us -> 166 us
  starting transfers between devices: 19.5 us -> 29 us
  blocking collectives: 98.3 us -> 105 us
    all_gather x1 -> x0, waiting for transfers between devices: 101 us -> none  [shards(): lax.all_gather(qkv_rows[:, 2 * D:], 'tm', axis=0, tiled=True)]
    all_gather x1, waiting for transfers between devices: 103 us -> 165 us  [shards(): lax.all_gather(qkv_rows[:, D:2 * D], 'tm', axis=0, tiled=True)]
    all_to_all x0 -> x1, starting transfers between devices: none -> 14.2 us  [shards(): lax.all_to_all(jnp.stack([qkv_rows[:, 2 * D:]] * lax.axis_size('tm')), 't...]
    psum x1, blocking collectives: 98.3 us -> 105 us  [shards(): sum_log, sum_act = lax.psum((local_log, local_act), ('space', 'tm'))]
  transfers between devices with their start and end apart: 4 -> 4, of which waited for: 2 -> 1; matrix products, arithmetic and copies ran while one was open for 11% -> 11% of each run, Pallas kernels for 0% -> 0%
where the time goes in v1:
time: 565 us; the launch traced here: 562 us
  waiting for transfers between devices  166 us (29%)
  local copies, waits for them, and re-layouts  157 us (28%)
  blocking collectives  105 us (19%)
  other arithmetic  49 us (9%)
  starting transfers between devices  29 us (5%)
  loops' own time  22.6 us (4%)
  between operations  16.8 us (3%)
  matrix products  16.2 us (3%)
    all_gather x1, waiting for transfers between devices, shards(): lax.all_gather(qkv_rows[:, D:2 * D], 'tm', axis=0, tiled=True)  165 us
    psum x1, blocking collectives, shards(): sum_log, sum_act = lax.psum((local_log, local_act), ('space', 'tm'))  105 us
    dynamic_slice x24, local copies, waits for them, and re-layouts, fold_rows(): lax.scan(visit_block, carry_in, (jnp.arange(row_total // BLK, dtype=jnp.i...  29.4 us
    another operation x1, loops' own time, fold_rows(): lax.scan(visit_block, carry_in, (jnp.arange(row_total // BLK, dtype=jnp.i...  21.8 us
    reduce_or x16, other arithmetic, visit_block(): needed = jnp.any(block_rows == block_id)  21.6 us
    concatenate x4, local copies, waits for them, and re-layouts, shards(): next_slab_field = jnp.concatenate([new_field[:, 1:], ahead_slab], axis=1)  15.3 us
    ppermute x2, starting transfers between devices, shifted(): lax.ppermute(x, axis, [(i, (i + by) % length) for i in range(length)])  14.8 us
    all_to_all x1, starting transfers between devices, shards(): lax.all_to_all(jnp.stack([qkv_rows[:, 2 * D:]] * lax.axis_size('tm')), 't...  14.2 us
  transfers between devices with their start and end apart: 4, of which 1 were waited for; matrix products, arithmetic and copies ran while one was open for 11% of the time, Pallas kernels for 0%

profile of v1, /device:TPU:1, one launch (start us, length us, event | category | flops | bytes accessed | tf_op | source)
XLA Modules:
  0.0 562.1 jit_solution(16625260063676555853)
XLA Ops:
  7.2 6.7 %reshape.276 = f32[4,4,8,4,16,4]{5,4,3,2,1,0:T(8,128)} reshape(f32[4,4,2048]{2,1,0:T(4,128)} %param.14) | data formatting | bytes 262144 | tf_op jit(solution)/shard_map/reshape | solution.py:110
  13.9 5.7 %copy.50 = f32[8,16,4,4,4,4]{1,0,5,4,3,2:T(8,128)} copy(f32[8,16,4,4,4,4]{5,1,4,0,3,2:T(8,128)} %bitcast.52) | data formatting | bytes 262144 | tf_op jit(solution)/shard_map/transpose | solution.py:112
  19.6 2.2 reshape.277
  28.9 3.2 stack.8
  32.2 14.2 %all-to-all-start = ((bf16[16,128,768]{1,2,0:T(8,128)(2,1)}), bf16[16,128,768]{1,2,0:T(8,128)(2,1)}, u32[]{:S(2)}, u32[]{:S(2)}) async-start(bf16[16,128,768]{1,2,0:T(8,128)(2,1)} %stack.8), calls=%async_computation | async-start | bytes 6291456 | tf_op jit(solution)/shard_map/all_to_all | solution.py:137
  47.7 1.7 copy.55
  51.7 165.4 %all-gather.2.cloned.1.call-done = bf16[2048,768]{1,0:T(8,128)(2,1)} async-done(((bf16[128,768]{1,0:T(8,128)(2,1)}), bf16[2048,768]{1,0:T(8,128)(2,1)}) %all-gather.2.cloned.1.call-update) | async-done | bytes 3145744 | tf_op jit(solution)/shard_map/all_gather | solution.py:135
  217.2 4.7 copy.54
  223.2 100.4 %while.16 = (s32[]{:T(128)}, f32[12,128]{1,0:T(8,128)S(1)}, f32[12,128]{1,0:T(8,128)S(1)}, f32[12,128,64]{1,2,0:T(8,128)}, s32[16]{0:T(128)}, /*index=5*/s32[1,8...) while((s32[]{:T(128)}, f32[12,128]{1,0:T(8,128)S(1)}, ...), condition=%wide.region_9.10_spmd, body=%wide.region_2.9_spmd.sunk | while | flops 52304800 | bytes 7768141 | solution.py:99
  227.2 4.5 conditional.2
  235.7 4.5 conditional.2
  244.2 4.5 conditional.2
  256.7 4.5 conditional.2
  269.3 4.5 conditional.2
  277.8 4.5 conditional.2
  290.3 4.5 conditional.2
  315.1 4.5 conditional.2
  323.6 1.8 broadcast_divide_fusion
  325.4 1.9 copy.56
  330.3 2.2 fusion.18
  334.2 2.2 reshape.280
  336.3 5.4 copy.60
  341.8 5.6 reshape.281
  347.4 4.3 reshape_reshape.3
  351.6 1.8 slice.74
  359.7 12.7 %collective-permute-start.1 = (bf16[4,1,2048]{2,1,0:T(2,128)(2,1)}, bf16[4,1,2048]{2,1,0:T(2,128)(2,1)}, u32[]{:S(2)}, u32[]{:S(2)}) collective-permute-start(bf16[4,1,2048]{2,1,0:T(2,128)(2,1)} %slice.87), channel_id=1, source_target_pairs={{0,496},{16,0},{32,16},{48,32},{64,48},{80,64},{96,80},{112,96},{1... | collective-permute-start | bytes 49160 | tf_op jit(solution)/shard_map/ppermute | solution.py:23
  372.4 2.5 copy.62
  375.0 2.4 convert_element_type.46
  377.4 2.1 collective-permute-start
  379.5 1.9 pad_maximum_fusion.1
  384.6 2.1 slice.68
  386.7 1.7 reshape.283
  388.4 4.4 reshape.285
  392.9 1.7 reshape.282
  394.6 4.5 reshape.284
  399.1 4.6 copy.61
  403.7 5.7 %copy.69 = f32[4,4,8,4,16,4]{4,2,5,3,1,0:T(8,128)} copy(f32[4,4,8,4,16,4]{5,4,3,2,1,0:T(8,128)} %reshape.285) | data formatting | bytes 262144 | tf_op jit(solution)/shard_map/reshape | solution.py:165
  409.4 5.6 %copy.68 = f32[4,4,8,4,16,4]{4,2,5,3,1,0:T(8,128)} copy(f32[4,4,8,4,16,4]{5,4,3,2,1,0:T(8,128)} %reshape.284) | data formatting | bytes 262144 | tf_op jit(solution)/shard_map/reshape | solution.py:164
  415.0 5.1 reshape.286
  420.1 4.6 copy.66
  425.4 2.1 concatenate.30
  427.5 2.8 copy.64
  431.7 2.8 concatenate.33
  434.5 2.8 copy.67
  437.3 3.7 fusion.5
  441.1 4.6 slice.55
  445.7 104.9 %all-reduce = (f32[]{:T(128)}, f32[]{:T(128)}) all-reduce(f32[]{:T(128)} %fusion.5, f32[]{:T(128)S(6)} %sub.78), channel_id=1, replica_groups=mesh['space'=32,'tm'=16] {'space','tm'}, use_global_device_ids=true, to_apply=%region_16.17 | all-reduce | flops 2 | bytes 16 | tf_op jit(solution)/shard_map/psum | solution.py:179
  553.2 2.1 fusion.20
  (201 shorter events, 106.3 us)
Async XLA Ops:
  7.2 18.5 %copy-start = (bf16[768,2304]{1,0:T(8,128)(2,1)S(1)}, bf16[768,2304]{1,0:T(8,128)(2,1)}, u32[]{:S(2)}) copy-start(bf16[768,2304]{1,0:T(8,128)(2,1)} %param.20) | copy-start | bytes 10616836
  7.2 16.2 %copy-start.6 = (s32[256]{0:T(256)}, s32[256]{0:T(256)S(1)}, u32[]{:S(2)}) copy-start(s32[256]{0:T(256)S(1)} %and_select_fusion.1) | copy-start | bytes 3076
  13.9 9.5 %copy-start.4 = (f32[768]{0:T(1024)S(1)}, f32[768]{0:T(1024)}, u32[]{:S(2)}) copy-start(f32[768]{0:T(1024)} %param.18) | copy-start | bytes 9220
  13.9 9.5 %copy-start.10 = (s32[1,1,128]{2,1,0:T(1,128)S(1)}, s32[1,1,128]{2,1,0:T(1,128)}, u32[]{:S(2)}) copy-start(s32[1,1,128]{2,1,0:T(1,128)} %param.15) | copy-start | bytes 1540
  13.9 11.7 %copy-start.9 = (f32[768]{0:T(1024)S(1)}, f32[768]{0:T(1024)}, u32[]{:S(2)}) copy-start(f32[768]{0:T(1024)} %param.19) | copy-start | bytes 9220
  24.9 0.8 copy-start.3
  32.1 14.9 %copy-start.8 = (s32[16,8]{0,1:T(8,128)S(1)}, s32[16,8]{0,1:T(8,128)}, u32[]{:S(2)}) copy-start(s32[16,8]{0,1:T(8,128)} %param.16) | copy-start | bytes 1540
  32.2 189.7 %all-to-all-start = ((bf16[16,128,768]{1,2,0:T(8,128)(2,1)}), bf16[16,128,768]{1,2,0:T(8,128)(2,1)}, u32[]{:S(2)}, u32[]{:S(2)}) async-start(bf16[16,128,768]{1,2,0:T(8,128)(2,1)} %stack.8), calls=%async_computation | async-start | bytes 6291456 | tf_op jit(solution)/shard_map/all_to_all | solution.py:137
  46.3 170.8 %all-gather.2.cloned.1.call-start = ((), (), s32[]{:S(2)}) async-start(), calls=%async_computation.1 | async-start | bytes 3342336 | tf_op jit(solution)/shard_map/all_gather | solution.py:135
  227.2 3.3 copy-start.1
  230.9 0.8 copy-start.2
  235.7 3.3 copy-start.1
  239.4 0.8 copy-start.2
  244.2 3.3 copy-start.1
  247.9 0.8 copy-start.2
  256.7 3.4 copy-start.1
  260.4 0.8 copy-start.2
  269.3 3.4 copy-start.1
  273.0 0.8 copy-start.2
  277.8 3.3 copy-start.1
  281.5 0.8 copy-start.2
  290.4 3.4 copy-start.1
  294.1 0.8 copy-start.2
  315.1 3.3 copy-start.1
  318.8 0.8 copy-start.2
  323.6 5.2 copy-start.5
  323.6 6.6 %copy-start.7 = (s32[256]{0:T(256)S(1)}, s32[256]{0:T(256)}, u32[]{:S(2)}) copy-start(s32[256]{0:T(256)} %copy-done.6) | copy-start | bytes 3076
  325.4 4.9 copy-start.11
  359.7 70.5 %collective-permute-start.1 = (bf16[4,1,2048]{2,1,0:T(2,128)(2,1)}, bf16[4,1,2048]{2,1,0:T(2,128)(2,1)}, u32[]{:S(2)}, u32[]{:S(2)}) collective-permute-start(bf16[4,1,2048]{2,1,0:T(2,128)(2,1)} %slice.87), channel_id=1, source_target_pairs={{0,496},{16,0},{32,16},{48,32},{64,48},{80,64},{96,80},{112,96},{1... | collective-permute-start | bytes 49160 | tf_op jit(solution)/shard_map/ppermute | solution.py:23
  377.4 48.0 %collective-permute-start = (bf16[1,4,2048]{2,1,0:T(4,128)(2,1)}, bf16[1,4,2048]{2,1,0:T(4,128)(2,1)S(1)}, u32[]{:S(2)}, u32[]{:S(2)}) collective-permute-start(bf16[1,4,2048]{2,1,0:T(4,128)(2,1)} %convert_element_type.46), channel_id=1, source_target_pairs={{0,15},{1,0},{2,1},{3,2},{4,3},{5,4},{6,5},{7,6},{8,7},{9,8},{10,9... | collective-permute-start | bytes 49160 | tf_op jit(solution)/shard_map/ppermute | solution.py:23
Sparse Core Ops, SparseCore 0:
  49.2 167.8 all-gather.1
